TPU v7x, 32 devices: a whole 2x2x4 slice. The times are simulated.
32 devices in a mesh: groups: 2 (over y), sec: 4 (over x, core), plane: 4 (over z).
Axes of the slice: x: 2, y: 2, z: 4, core: 2. Of those that a mesh axis runs over, the one named last changes fastest.
Arguments:
- tokens: bfloat16 [16, 512, 1024], P(('groups', 'sec'), 'plane'), parts along dimension 0, may hold values from -8 to 8
- counts: int32 [16], P('groups'), parts along dimension 0, may hold values from 128 to 512, as said below
- region_ids: int32 [16, 512], P(('groups', 'sec'), 'plane'), parts along dimension 0, may hold values from 0 to 31
- norm_gains: float32 [2, 1024], replicated, may hold values from 0.1 to 1.9
- cross_qkv: bfloat16 [1024, 3072], P('plane'), may hold values from -2 to 2
- cross_out: bfloat16 [1024, 1024], P('plane'), may hold values from -0.1875 to 0.1875
- plane_qkv: bfloat16 [1024, 3072], P('plane'), may hold values from -2 to 2
- plane_out: bfloat16 [1024, 1024], P('plane'), may hold values from -0.1875 to 0.1875
Outputs:
- encoded: bfloat16 [16, 512, 1024], P(('groups', 'sec'), 'plane'), parts along dimension 0
- pooled: float32 [64, 1024], P(('groups', 'sec', 'plane')), parts along dimension 0
There are 2 independent parts, one for each index of `groups`. A program takes and returns all parts, laid end to end along the dimension named above; an argument that names none is the same for every part. Nothing has to cross between parts.
Inputs may be any that keep to these rules, and one draw needn't show every extreme that they name: `counts`: valid tissue tokens of each section; they are the first positions of the section.
All inputs are finite; a program needn't handle non-finite values.
Results may differ from a plain program's by a relative error of at most 0.009.
Values may be sent and summed in bfloat16 or wider, within the bound.
No kernel may reach another device: no remote copies, remote signals or barrier semaphores. Data moves between devices by JAX's collectives and lax.ppermute only.
A program may use at most 64 MiB of HBM per device.

v0:
```python
import math
import jax
import jax.numpy as jnp
from jax import lax
from jax.sharding import PartitionSpec as P

HEADS = 16
HEAD_DIM = 64
WINDOW = 128
negative_big = -1e30


def shifted_2(value, axis, by):
    peers = lax.axis_size(axis)
    pairs = [(i, i + by) for i in range(peers) if 0 <= i + by < peers]
    return lax.ppermute(value, axis, pairs)


def rms_norm(values, gain):
    wide = values.astype(jnp.float32)
    scaled = wide * lax.rsqrt(jnp.mean(wide * wide, axis=-1, keepdims=True) + 1e-06) * gain
    return scaled.astype(jnp.bfloat16)


def masked_softmax(scores, allowed):
    shifted = jnp.where(allowed, scores, negative_big)
    top = jnp.max(shifted, axis=-1, keepdims=True)
    expo = jnp.where(allowed, jnp.exp(shifted - top), 0.0)
    return (expo / jnp.sum(expo, axis=-1, keepdims=True)).astype(jnp.bfloat16)


def fold_product(inputs, weight_piece):
    return jnp.dot(inputs, weight_piece, preferred_element_type=jnp.float32)


def attend_items(pieces):
    packed_all, flags_all = pieces
    seq_len = packed_all.shape[2]
    block_len = 512
    score_scale = 1.0 / math.sqrt(HEAD_DIM)
    key_index = jnp.arange(seq_len, dtype=jnp.int32)

    def one_item(item_pair):
        packed, key_flag = item_pair
        key_rows = packed[:, HEAD_DIM : 2 * HEAD_DIM]
        value_rows = packed[:, 2 * HEAD_DIM :]
        key_alive = key_flag > 0.5
        query_blocks = packed[:, :HEAD_DIM].reshape(seq_len // block_len, block_len, HEAD_DIM)
        block_starts = jnp.arange(seq_len // block_len, dtype=jnp.int32) * block_len

        def one_block(block_pair):
            query_rows, offset = block_pair
            scores = (
                jnp.einsum("qd,kd->qk", query_rows, key_rows, preferred_element_type=jnp.float32)
                * score_scale
            )
            own_index = offset + jnp.arange(block_len, dtype=jnp.int32)
            allowed = key_alive[None, :] | (key_index[None, :] == own_index[:, None])
            attention = masked_softmax(scores, allowed)
            return jnp.dot(attention, value_rows, preferred_element_type=jnp.float32).astype(
                jnp.bfloat16
            )

        return lax.map(one_block, (query_blocks, block_starts)).reshape(seq_len, HEAD_DIM)

    return lax.map(one_item, (packed_all[0], flags_all[0]))[None]


def body(tokens, counts, region_ids, norm_gains, cross_qkv, cross_out, plane_qkv, plane_out):
    sec_block, tok_block, model_width = tokens.shape
    plane_count = lax.axis_size("plane")
    regions = 2 * lax.axis_size("sec") * plane_count
    positions = lax.axis_index("plane") * tok_block + jnp.arange(tok_block, dtype=jnp.int32)
    padded_counts = jnp.concatenate(
        [jnp.zeros((1,), jnp.int32), counts, jnp.zeros((1,), jnp.int32)]
    )
    near_counts = lax.dynamic_slice_in_dim(
        padded_counts, lax.axis_index("sec") * sec_block, sec_block + 2
    )
    near_valid = positions[None, :] < near_counts[:, None]
    own_valid = near_valid[1 : sec_block + 1]
    score_scale = 1.0 / math.sqrt(HEAD_DIM)
    normed = rms_norm(tokens, norm_gains[0])
    inputs = normed.reshape(-1, model_width)
    result = fold_product(inputs, lax.all_gather(cross_qkv, "plane", axis=0, tiled=True))
    projected = result.astype(jnp.bfloat16).reshape(sec_block, tok_block, 3 * model_width)
    own_kv = projected[:, :, model_width:]
    from_below = shifted_2(own_kv[sec_block - 1], "sec", 1)
    from_above = shifted_2(own_kv[0], "sec", -1)
    near_kv = jnp.concatenate([from_below[None], own_kv, from_above[None]], axis=0)
    queries = projected[:, :, :model_width]
    windows = tok_block // WINDOW
    query_win = queries.reshape(sec_block, windows, WINDOW, HEADS, HEAD_DIM)
    pair_win = near_kv.reshape(sec_block + 2, windows, WINDOW, 2, HEADS, HEAD_DIM)
    stacked = jnp.concatenate(
        [pair_win[0:sec_block], pair_win[1 : sec_block + 1], pair_win[2 : sec_block + 2]], axis=2
    )
    valid_win = near_valid.reshape(sec_block + 2, windows, WINDOW)
    valid_three = jnp.concatenate(
        [valid_win[0:sec_block], valid_win[1 : sec_block + 1], valid_win[2 : sec_block + 2]], axis=2
    )
    itself = jnp.arange(3 * WINDOW)[None, :] == jnp.arange(WINDOW)[:, None] + WINDOW
    scores = (
        jnp.einsum(
            "snqhd,snkhd->snhqk", query_win, stacked[:, :, :, 0], preferred_element_type=jnp.float32
        )
        * score_scale
    )
    allowed = valid_three[:, :, None, None, :] | itself[None, None, None]
    attention = masked_softmax(scores, allowed)
    context = jnp.einsum(
        "snhqk,snkhd->snqhd", attention, stacked[:, :, :, 1], preferred_element_type=jnp.float32
    )
    context = context.astype(jnp.bfloat16).reshape(-1, model_width)
    result = fold_product(context, lax.all_gather(cross_out, "plane", axis=0, tiled=True))
    after_cross = (tokens.reshape(-1, model_width).astype(jnp.float32) + result).astype(
        jnp.bfloat16
    )
    normed = rms_norm(after_cross, norm_gains[1])
    result = fold_product(normed, lax.all_gather(plane_qkv, "plane", axis=0, tiled=True))
    projected = result.astype(jnp.bfloat16).reshape(sec_block, tok_block, 3, HEADS, HEAD_DIM)
    per_device = sec_block * HEADS // plane_count
    heads_first = jnp.transpose(projected, (0, 3, 1, 2, 4)).reshape(
        plane_count, per_device, tok_block, 3 * HEAD_DIM
    )
    key_flags = jnp.broadcast_to(own_valid[:, None, :], (sec_block, HEADS, tok_block)).astype(
        jnp.bfloat16
    )
    key_flags = key_flags.reshape(plane_count, per_device, tok_block)
    attended = attend_items(
        (
            lax.all_to_all(heads_first, "plane", split_axis=0, concat_axis=2, tiled=True),
            lax.all_to_all(key_flags, "plane", split_axis=0, concat_axis=2, tiled=True),
        )
    )
    returned = lax.all_to_all(attended, "plane", split_axis=2, concat_axis=0, tiled=True)
    context = jnp.transpose(
        returned.reshape(sec_block, HEADS, tok_block, HEAD_DIM), (0, 2, 1, 3)
    ).reshape(-1, model_width)
    result = fold_product(context, lax.all_gather(plane_out, "plane", axis=0, tiled=True))
    encoded = (after_cross.astype(jnp.float32) + result).astype(jnp.bfloat16)
    labels = region_ids.reshape(-1)
    member = (jnp.arange(regions, dtype=jnp.int32)[:, None] == labels[None, :]) & own_valid.reshape(
        -1
    )[None, :]
    region_sum = jnp.dot(member.astype(jnp.bfloat16), encoded, preferred_element_type=jnp.float32)
    region_count = jnp.sum(member.astype(jnp.float32), axis=1)
    totals, counted = (
        lax.psum_scatter(region_sum, ("sec", "plane"), scatter_dimension=0, tiled=True),
        lax.psum_scatter(region_count, ("sec", "plane"), scatter_dimension=0, tiled=True),
    )
    pooled = totals / jnp.maximum(counted, 1.0)[:, None]
    return (encoded.reshape(sec_block, tok_block, model_width), pooled)


def solution(mesh):
    in_specs = (
        P(("groups", "sec"), "plane", None),
        P("groups"),
        P(("groups", "sec"), "plane"),
        P(),
        P("plane", None),
        P("plane", None),
        P("plane", None),
        P("plane", None),
    )
    out_specs = (P(("groups", "sec"), "plane", None), P(("groups", "sec", "plane"), None))
    return jax.shard_map(body, mesh=mesh, in_specs=in_specs, out_specs=out_specs, check_vma=False)
```

profile of v0, /device:TPU:8, one launch (start us, length us, event | category | flops | bytes accessed | tf_op | source)
XLA Modules:
  0.0 521.9 jit_solution(6824321501404920193)
XLA Ops:
  7.2 0.7 all-gather.5.cloned.1.call-update
  8.0 0.7 all-gather.7.cloned.1.call-update
  8.7 0.7 all-gather.9.cloned.1.call-update
  10.1 113.1 %all-gather.5.cloned.1.call-done = bf16[1024,3072]{1,0:T(8,128)(2,1)} async-done(((bf16[256,3072]{1,0:T(8,128)(2,1)}), bf16[1024,3072]{1,0:T(8,128)(2,1)}) %all-gather.5.cloned.1.call-update) | async-done | bytes 6291472 | tf_op jit(solution)/shard_map/all_gather | solution.py:85
  123.2 4.6 convolution_convert_fusion.2
  127.8 1.0 copy.72
  128.8 2.7 collective-permute-start
  131.5 1.0 copy.74
  132.6 1.3 collective-permute-start.1
  134.1 0.8 slice.101
  135.0 0.7 copy.73
  135.6 1.3 copy.58
  137.2 1.4 pad_maximum_fusion.2
  138.6 0.5 pad_maximum_fusion
  139.1 1.0 fusion.18
  140.1 3.2 fusion.43
  143.4 1.8 fusion.22
  145.2 0.5 copy.59
  145.8 24.5 %all-gather.7.cloned.1.call-done = bf16[1024,1024]{1,0:T(8,128)(2,1)} async-done(((bf16[256,1024]{1,0:T(8,128)(2,1)}), bf16[1024,1024]{1,0:T(8,128)(2,1)}) %all-gather.7.cloned.1.call-update) | async-done | bytes 2097168 | tf_op jit(solution)/shard_map/all_gather | solution.py:115
  170.3 2.4 fusion.23
  172.8 111.8 %all-gather.9.cloned.1.call-done = bf16[1024,3072]{1,0:T(8,128)(2,1)} async-done(((bf16[256,3072]{1,0:T(8,128)(2,1)}), bf16[1024,3072]{1,0:T(8,128)(2,1)}) %all-gather.9.cloned.1.call-update) | async-done | bytes 6291472 | tf_op jit(solution)/shard_map/all_gather | solution.py:120
  284.6 5.8 %convolution_convert_fusion.1 = bf16[256,3072]{1,0:T(8,128)(2,1)} fusion(bf16[1024,3072]{1,0:T(8,128)(2,1)} %all-gather.9.cloned.1.call-done, bf16[256,1024]{1,0:T(8,128)(2,1)S(1)} %get-tuple-element.97, f32[1024]{0:T(1024)S(1)} %bitcast.126, f32[256]{0:T(256)S(1)} %add_rsqrt_fusion), kind=kOutput, calls=%fused_computation.23 | convolution fusion | flops 1612447744 | bytes 8393728 | tf_op jit(solution)/shard_map/dot_general | solution.py:33
  290.4 1.7 copy.60
  292.1 0.4 reshape.152
  292.5 0.4 copy.61
  293.0 41.6 %all_to_all.45 = bf16[4,8,128,192]{2,3,1,0:T(8,128)(2,1)S(1)} all-to-all(bf16[4,8,128,192]{2,3,1,0:T(8,128)(2,1)S(1)} %bitcast.105), channel_id=1, replica_groups=mesh['groups'=2,'sec'=4,'plane'=4] {'plane'}, dimensions={0} | all-to-all | bytes 3145728 | tf_op jit(solution)/shard_map/all_to_all | solution.py:132
  334.6 0.6 broadcast_in_dim.86
  335.2 5.0 all-to-all-start
  340.2 0.6 all-gather.11.cloned.1.call-update
  340.8 2.5 copy.69
  343.3 1.1 all-to-all-done
  344.4 16.5 %while.11 = (s32[]{:T(128)}, bf16[8,512,64]{1,2,0:T(8,128)(2,1)S(1)}, bf16[8,512]{1,0:T(8,128)(2,1)S(1)}, bf16[8,512,192]{2,1,0:T(8,128)(2,1)}, s32[]{:T(128)}) while((s32[]{:T(128)}, bf16[8,512,64]{1,2,0:T(8,128)(2,1)S(1)}, bf16[8,512]{1,0:T(8,128)(2,1)S(1)}, bf16[8,512,192]{2,1,0:T(8,128)(2,1)}, s32[]{:T(128)}) %tuple.56), condition=%wide.region_7.8_spmd.clone, body=%wide.region_4.7_spmd.clone.sunk | while | flops 71336448 | bytes 3945545 | solution.py:66
  344.4 1.0 dynamic-slice_bitcast_fusion.2
  345.4 0.4 fusion.56
  346.0 0.4 fusion.58
  346.5 1.0 dynamic-slice_bitcast_fusion.2
  348.1 0.4 fusion.58
  348.5 1.0 dynamic-slice_bitcast_fusion.2
  350.1 0.4 fusion.58
  350.6 1.0 dynamic-slice_bitcast_fusion.2
  352.2 0.4 fusion.58
  352.7 1.0 dynamic-slice_bitcast_fusion.2
  353.6 0.4 fusion.56
  354.3 0.4 fusion.58
  354.7 1.0 dynamic-slice_bitcast_fusion.2
  355.7 0.4 fusion.56
  356.3 0.4 fusion.58
  356.8 1.0 dynamic-slice_bitcast_fusion.2
  357.8 0.4 fusion.56
  358.4 0.4 fusion.58
  358.9 1.0 dynamic-slice_bitcast_fusion.2
  360.5 0.4 fusion.58
  360.9 0.8 copy.64
  361.8 1.6 reshape.161
  363.3 5.0 all-to-all-start.2
  368.3 0.6 dynamic-slice.1
  369.7 48.3 %all-reduce.1 = f32[32]{0:T(128)S(1)} all-reduce(f32[32]{0:T(128)S(1)} %convert_reduce_fusion), channel_id=3, replica_groups=mesh['groups'=2,'sec'=4,'plane'=4] {'sec','plane'}, use_global_device_ids=true, to_apply=%region_10.11.clone | all-reduce | flops 32 | bytes 256
  418.0 0.7 reshape.162
  418.7 0.8 copy.70
  419.7 0.5 copy.67
  420.3 2.3 fusion.19
  422.6 0.8 fusion.34
  423.6 90.4 %all-reduce.4.cloned.1.call-done = f32[32,1024]{1,0:T(8,128)} async-done(((f32[32,1024]{1,0:T(8,128)}), f32[32,1024]{1,0:T(8,128)}) %all-reduce.4.cloned.1.call-update) | async-done | bytes 131088
  514.0 1.4 dynamic-slice_divide_fusion
  (68 shorter events, 5.5 us)
Async XLA Ops:
  7.2 2.3 copy-start.6
  7.2 2.5 copy-start
  7.2 2.7 copy-start.4
  7.2 116.0 %all-gather.5.cloned.1.call-start = ((), (), s32[]{:S(2)}) async-start(), calls=%async_computation.3 | async-start | bytes 7864320 | tf_op jit(solution)/shard_map/all_gather | solution.py:85
  7.9 162.4 %all-gather.7.cloned.1.call-start = ((), (), s32[]{:S(2)}) async-start(), calls=%async_computation.4 | async-start | bytes 2621440 | tf_op jit(solution)/shard_map/all_gather | solution.py:115
  8.7 275.9 %all-gather.9.cloned.1.call-start = ((), (), s32[]{:S(2)}) async-start(), calls=%async_computation.5 | async-start | bytes 7864320 | tf_op jit(solution)/shard_map/all_gather | solution.py:120
  128.8 8.1 %collective-permute-start = (bf16[128,2048]{0,1:T(8,128)(2,1)}, bf16[128,2048]{0,1:T(8,128)(2,1)}, u32[]{:S(2)}, u32[]{:S(2)}) collective-permute-start(bf16[128,2048]{0,1:T(8,128)(2,1)} %bitcast.121), channel_id=1, source_target_pairs={{0,4},{4,8},{8,12},{1,5},{5,9},{9,13},{2,6},{6,10},{10,14},{3,7},{... | collective-permute-start | bytes 1572872 | tf_op jit(solution)/shard_map/ppermute | solution.py:16
  132.6 4.7 collective-permute-start.1
  172.7 117.7 %copy-start.2 = (bf16[256,1024]{1,0:T(8,128)(2,1)}, bf16[256,1024]{1,0:T(8,128)(2,1)S(1)}, u32[]{:S(2)}) copy-start(bf16[256,1024]{1,0:T(8,128)(2,1)S(1)} %get-tuple-element.97) | copy-start | bytes 1572868
  335.2 9.2 %all-to-all-start = ((bf16[4,8,128]{2,1,0:T(8,128)(2,1)}), bf16[4,8,128]{2,1,0:T(8,128)(2,1)S(1)}, u32[]{:S(2)}, u32[]{:S(2)}) async-start(bf16[4,8,128]{2,1,0:T(8,128)(2,1)} %broadcast_in_dim.86), calls=%async_computation | async-start | bytes 16384 | tf_op jit(solution)/shard_map/all_to_all | solution.py:133
  340.2 80.1 %all-gather.11.cloned.1.call-start = ((), (), s32[]{:S(2)}) async-start(), calls=%async_computation.6 | async-start | bytes 2621440 | tf_op jit(solution)/shard_map/all_gather | solution.py:140
  360.9 7.4 %copy-start.7 = (u32[32]{0:T(128)S(1)}, u32[32]{0:T(128)}, u32[]{:S(2)}) copy-start(u32[32]{0:T(128)} %constant.80) | copy-start | bytes 388
  360.9 8.7 %copy-start.5 = (s32[2,128]{1,0:T(2,128)S(1)}, s32[2,128]{1,0:T(2,128)}, u32[]{:S(2)}) copy-start(s32[2,128]{1,0:T(2,128)} %param.12) | copy-start | bytes 3076
  363.3 56.9 %copy-start.3 = (bf16[256,1024]{1,0:T(8,128)(2,1)S(1)}, bf16[256,1024]{1,0:T(8,128)(2,1)}, u32[]{:S(2)}) copy-start(bf16[256,1024]{1,0:T(8,128)(2,1)} %copy-done.2) | copy-start | bytes 1572868
  363.3 54.7 %all-to-all-start.2 = ((bf16[4,2,32768]{2,1,0:T(2,128)(2,1)}), bf16[4,2,32768]{2,1,0:T(2,128)(2,1)S(1)}, u32[]{:S(2)}, u32[]{:S(2)}) async-start(bf16[4,2,32768]{2,1,0:T(2,128)(2,1)} %reshape.161), calls=%async_computation.2 | async-start | bytes 1048576 | tf_op jit(solution)/shard_map/all_to_all | solution.py:136
  368.3 145.6 %all-reduce.4.cloned.1.call-start = ((), (), s32[]{:S(2)}) async-start(), calls=%async_computation.7 | async-start | bytes 262144
  422.6 92.8 %copy-start.1 = (bf16[256,1024]{1,0:T(8,128)(2,1)}, bf16[256,1024]{1,0:T(8,128)(2,1)S(1)}, u32[]{:S(2)}) copy-start(bf16[256,1024]{1,0:T(8,128)(2,1)S(1)} %fusion.19) | copy-start | bytes 1572868
Sparse Core Ops, SparseCore 0:
  9.6 113.5 all-gather.4
  124.7 45.5 all-gather.6
  171.9 112.6 all-gather.8
  342.3 54.9 all-gather.10
  423.6 90.2 all-reduce.3
where the time goes:
time: 523 us; the launch traced here: 522 us
  waiting for transfers between devices  344 us (66%)
  blocking collectives  89.9 us (17%)
  matrix products  25.1 us (5%)
  local copies, waits for them, and re-layouts  24.3 us (5%)
  between operations  14.8 us (3%)
  starting transfers between devices  14.1 us (3%)
  other arithmetic  9.64 us (2%)
    all_gather x1, waiting for transfers between devices, body(): lax.all_gather(cross_qkv, 'plane', axis=0, tiled=True)  113 us
    all_gather x1, waiting for transfers between devices, body(): lax.all_gather(plane_qkv, 'plane', axis=0, tiled=True)  112 us
    unnamed x6, waiting for transfers between devices  93 us
    unnamed x1, blocking collectives  48.3 us
    all_to_all x1, blocking collectives, body(): lax.all_to_all(heads_first, 'plane', split_axis=0, concat_axis=2, tiled=T...  41.6 us
    all_gather x1, waiting for transfers between devices, body(): lax.all_gather(cross_out, 'plane', axis=0, tiled=True)  24.5 us
    dot_general x4, matrix products, fold_product(): return jnp.dot(inputs, weight_piece, preferred_element_type=jnp.float32)  15.1 us
  transfers between devices with their start and end apart: 9, of which 6 were waited for; matrix products, arithmetic and copies ran while one was open for 9% of the time, Pallas kernels for 0%

commit v1 on v0

--- a/solution.py
+++ b/solution.py
@@ -8,6 +8,22 @@
 HEAD_DIM = 64
 WINDOW = 128
 negative_big = -1e30
+
+
+def collect(x, axis, dim):
+    ways, here, step = (lax.axis_size(axis), lax.axis_index(axis), x.shape[dim])
+    lengths = [n * ways if d == dim else n for d, n in enumerate(x.shape)]
+    full = lax.dynamic_update_slice_in_dim(jnp.zeros(lengths, x.dtype), x, here * step, axis=dim)
+    going_up = going_down = x
+    for far in range(1, ways // 2 + 1):
+        going_up = lax.ppermute(going_up, axis, [(d, (d + 1) % ways) for d in range(ways)])
+        full = lax.dynamic_update_slice_in_dim(full, going_up, (here - far) % ways * step, axis=dim)
+        if 2 * far < ways:
+            going_down = lax.ppermute(going_down, axis, [(d, (d - 1) % ways) for d in range(ways)])
+            full = lax.dynamic_update_slice_in_dim(
+                full, going_down, (here + far) % ways * step, axis=dim
+            )
+    return full
 
 
 def shifted_2(value, axis, by):
@@ -82,7 +98,7 @@
     score_scale = 1.0 / math.sqrt(HEAD_DIM)
     normed = rms_norm(tokens, norm_gains[0])
     inputs = normed.reshape(-1, model_width)
-    result = fold_product(inputs, lax.all_gather(cross_qkv, "plane", axis=0, tiled=True))
+    result = fold_product(inputs, collect(cross_qkv, "plane", 0))
     projected = result.astype(jnp.bfloat16).reshape(sec_block, tok_block, 3 * model_width)
     own_kv = projected[:, :, model_width:]
     from_below = shifted_2(own_kv[sec_block - 1], "sec", 1)

time: 523 us -> 484 us (0.925)
  waiting for transfers between devices: 344 us -> 282 us
  starting transfers between devices: 14.1 us -> 36.4 us
    ppermute x0 -> x3, waiting for transfers between devices: none -> 180 us  [the longest x2 173 us: collect(): lax.ppermute(going_up, axis, [(d, (d + 1) % ways) for d in range(ways)])]
    all_gather x1 -> x0, waiting for transfers between devices: 113 us -> none  [body(): lax.all_gather(cross_qkv, 'plane', axis=0, tiled=True)]
    all_gather x1, waiting for transfers between devices: 112 us -> 8.1 us  [body(): lax.all_gather(plane_qkv, 'plane', axis=0, tiled=True)]
    all_gather x1, waiting for transfers between devices: 24.5 us -> 0.02 us  [body(): lax.all_gather(cross_out, 'plane', axis=0, tiled=True)]
    ppermute x0 -> x3, starting transfers between devices: none -> 22.8 us  [the longest x2 22.4 us: collect(): lax.ppermute(going_up, axis, [(d, (d + 1) % ways) for d in range(ways)])]
    unnamed x6 -> x5, waiting for transfers between devices: 93 us -> 91.5 us
  transfers between devices with their start and end apart: 9 -> 11, of which waited for: 6 -> 7; matrix products, arithmetic and copies ran while one was open for 9% -> 10% of each run, Pallas kernels for 0% -> 0%
where the time goes in v1:
time: 484 us; the launch traced here: 483 us
  waiting for transfers between devices  282 us (58%)
  blocking collectives  88.8 us (18%)
  starting transfers between devices  36.4 us (8%)
  local copies, waits for them, and re-layouts  26.1 us (5%)
  matrix products  22.4 us (5%)
  between operations  14.9 us (3%)
  other arithmetic  12.4 us (3%)
    ppermute x2, waiting for transfers between devices, collect(): lax.ppermute(going_up, axis, [(d, (d + 1) % ways) for d in range(ways)])  173 us
    unnamed x5, waiting for transfers between devices  91.5 us
    unnamed x1, blocking collectives  48.5 us
    all_to_all x1, blocking collectives, body(): lax.all_to_all(heads_first, 'plane', split_axis=0, concat_axis=2, tiled=T...  40.3 us
    ppermute x2, starting transfers between devices, collect(): lax.ppermute(going_up, axis, [(d, (d + 1) % ways) for d in range(ways)])  22.4 us
    dot_general x4, matrix products, fold_product(): return jnp.dot(inputs, weight_piece, preferred_element_type=jnp.float32)  12.4 us
  transfers between devices with their start and end apart: 11, of which 7 were waited for; matrix products, arithmetic and copies ran while one was open for 10% of the time, Pallas kernels for 0%

profile of v1, /device:TPU:8, one launch (start us, length us, event | category | flops | bytes accessed | tf_op | source)
XLA Modules:
  0.0 483.1 jit_solution(2244698668681559025)
XLA Ops:
  7.2 0.7 all-gather.4.cloned.1.call-update
  8.0 0.7 all-gather.6.cloned.1.call-update
  8.7 1.6 collective-permute-start
  10.3 0.4 collective-permute-start.1
  10.7 0.7 pad_add_fusion
  11.6 1.2 multiply_reduce_fusion
  12.9 0.8 fusion.42
  13.7 81.8 %collective-permute-done = bf16[256,3072]{1,0:T(8,128)(2,1)S(1)} collective-permute-done((bf16[256,3072]{1,0:T(8,128)(2,1)}, bf16[256,3072]{1,0:T(8,128)(2,1)S(1)}, u32[]{:S(2)}, u32[]{:S(2)}) %collective-permute-start) | collective-permute-done | bytes 1572896 | tf_op jit(solution)/shard_map/ppermute | solution.py:19
  95.6 20.7 %collective-permute-start.2 = (bf16[256,3072]{1,0:T(8,128)(2,1)S(1)}, bf16[256,3072]{1,0:T(8,128)(2,1)S(1)}, u32[]{:S(2)}, u32[]{:S(2)}) collective-permute-start(bf16[256,3072]{1,0:T(8,128)(2,1)S(1)} %collective-permute-done), channel_id=1, source_target_pairs={{0,1},{1,2},{2,3},{3,0},{4,5},{5,6},{6,7},{7,4},{8,9},{9,10},{10,1... | collective-permute-start | bytes 4718600 | tf_op jit(solution)/shard_map/ppermute | solution.py:19
  116.3 1.2 multiply_convert_fusion
  117.5 0.8 broadcast_in_dim.81
  118.7 6.2 %collective-permute-done.1 = bf16[256,3072]{1,0:T(8,128)(2,1)} collective-permute-done((bf16[256,3072]{1,0:T(8,128)(2,1)}, bf16[256,3072]{1,0:T(8,128)(2,1)}, u32[]{:S(2)}, u32[]{:S(2)}) %collective-permute-start.1) | collective-permute-done | bytes 1572896 | tf_op jit(solution)/shard_map/ppermute | solution.py:22
  124.9 1.6 constant_dynamic-update-slice_fusion.1
  126.5 91.5 %collective-permute-done.2 = bf16[256,3072]{1,0:T(8,128)(2,1)S(1)} collective-permute-done((bf16[256,3072]{1,0:T(8,128)(2,1)S(1)}, bf16[256,3072]{1,0:T(8,128)(2,1)S(1)}, u32[]{:S(2)}, u32[]{:S(2)}) %collective-permute-start.2) | collective-permute-done | bytes 1572896 | tf_op jit(solution)/shard_map/ppermute | solution.py:19
  218.2 1.8 convolution_convert_fusion.2
  220.2 1.0 copy.72
  221.2 2.1 collective-permute-start.3
  223.3 1.0 copy.74
  224.3 1.5 collective-permute-start.4
  226.0 0.7 copy.73
  227.0 1.8 collective-permute-done.4
  228.8 1.4 pad_maximum_fusion.2
  230.2 0.5 pad_maximum_fusion
  230.7 1.0 fusion.18
  231.7 3.2 fusion.43
  235.0 1.8 fusion.22
  236.8 0.5 copy.59
  237.4 2.4 fusion.23
  239.9 8.1 %all-gather.6.cloned.1.call-done = bf16[1024,3072]{1,0:T(8,128)(2,1)} async-done(((bf16[256,3072]{1,0:T(8,128)(2,1)}), bf16[1024,3072]{1,0:T(8,128)(2,1)}) %all-gather.6.cloned.1.call-update) | async-done | bytes 6291472 | tf_op jit(solution)/shard_map/all_gather | solution.py:136
  248.0 5.8 %convolution_convert_fusion.1 = bf16[256,3072]{1,0:T(8,128)(2,1)} fusion(bf16[1024,3072]{1,0:T(8,128)(2,1)} %all-gather.6.cloned.1.call-done, bf16[256,1024]{1,0:T(8,128)(2,1)S(1)} %get-tuple-element.97, f32[1024]{0:T(1024)S(1)} %bitcast.125, f32[256]{0:T(256)S(1)} %add_rsqrt_fusion), kind=kOutput, calls=%fused_computation.23 | convolution fusion | flops 1612447744 | bytes 8393728 | tf_op jit(solution)/shard_map/dot_general | solution.py:49
  253.8 1.7 copy.60
  255.5 0.4 reshape.152
  256.3 40.3 %all_to_all.45 = bf16[4,8,128,192]{2,3,1,0:T(8,128)(2,1)S(1)} all-to-all(bf16[4,8,128,192]{2,3,1,0:T(8,128)(2,1)S(1)} %bitcast.105), channel_id=1, replica_groups=mesh['groups'=2,'sec'=4,'plane'=4] {'plane'}, dimensions={0} | all-to-all | bytes 3145728 | tf_op jit(solution)/shard_map/all_to_all | solution.py:148
  296.7 0.6 broadcast_in_dim.90
  297.3 5.0 %all-to-all-start = ((bf16[4,8,128]{2,1,0:T(8,128)(2,1)}), bf16[4,8,128]{2,1,0:T(8,128)(2,1)S(1)}, u32[]{:S(2)}, u32[]{:S(2)}) async-start(bf16[4,8,128]{2,1,0:T(8,128)(2,1)} %broadcast_in_dim.90), calls=%async_computation | async-start | bytes 16384 | tf_op jit(solution)/shard_map/all_to_all | solution.py:149
  302.3 0.7 all-gather.8.cloned.1.call-update
  303.0 2.6 copy.69
  305.6 0.9 all-to-all-done
  306.5 16.5 %while.11 = (s32[]{:T(128)}, bf16[8,512,64]{1,2,0:T(8,128)(2,1)S(1)}, bf16[8,512]{1,0:T(8,128)(2,1)S(1)}, bf16[8,512,192]{2,1,0:T(8,128)(2,1)}, s32[]{:T(128)}) while((s32[]{:T(128)}, bf16[8,512,64]{1,2,0:T(8,128)(2,1)S(1)}, bf16[8,512]{1,0:T(8,128)(2,1)S(1)}, bf16[8,512,192]{2,1,0:T(8,128)(2,1)}, s32[]{:T(128)}) %tuple.54), condition=%wide.region_7.8_spmd.clone, body=%wide.region_4.7_spmd.clone.sunk | while | flops 71336448 | bytes 3945545 | solution.py:82
  306.5 1.0 dynamic-slice_bitcast_fusion.2
  308.1 0.4 fusion.58
  308.6 1.0 dynamic-slice_bitcast_fusion.2
  310.1 0.4 fusion.58
  310.6 1.0 dynamic-slice_bitcast_fusion.2
  312.2 0.4 fusion.58
  312.7 1.0 dynamic-slice_bitcast_fusion.2
  314.3 0.4 fusion.58
  314.7 1.0 dynamic-slice_bitcast_fusion.2
  316.3 0.4 fusion.58
  316.8 1.0 dynamic-slice_bitcast_fusion.2
  318.9 1.0 dynamic-slice_bitcast_fusion.2
  320.9 1.0 dynamic-slice_bitcast_fusion.2
  323.0 0.8 copy.64
  323.9 1.6 reshape.161
  325.4 4.9 %all-to-all-start.2 = ((bf16[4,2,32768]{2,1,0:T(2,128)(2,1)}), bf16[4,2,32768]{2,1,0:T(2,128)(2,1)S(1)}, u32[]{:S(2)}, u32[]{:S(2)}) async-start(bf16[4,2,32768]{2,1,0:T(2,128)(2,1)} %reshape.161), calls=%async_computation.2 | async-start | bytes 1048576 | tf_op jit(solution)/shard_map/all_to_all | solution.py:152
  330.3 0.6 dynamic-slice.1
  331.7 48.5 %all-reduce.1 = f32[32]{0:T(128)S(1)} all-reduce(f32[32]{0:T(128)S(1)} %convert_reduce_fusion), channel_id=3, replica_groups=mesh['groups'=2,'sec'=4,'plane'=4] {'sec','plane'}, use_global_device_ids=true, to_apply=%region_10.11.clone | all-reduce | flops 32 | bytes 256
  380.2 0.7 reshape.162
  380.9 0.8 copy.70
  381.9 0.5 copy.67
  382.5 2.3 fusion.19
  384.8 0.9 fusion.34
  385.8 89.4 %all-reduce.4.cloned.1.call-done = f32[32,1024]{1,0:T(8,128)} async-done(((f32[32,1024]{1,0:T(8,128)}), f32[32,1024]{1,0:T(8,128)}) %all-reduce.4.cloned.1.call-update) | async-done | bytes 131088
  475.2 1.4 dynamic-slice_divide_fusion
  (74 shorter events, 8.7 us)
Async XLA Ops:
  7.2 111.1 %copy-start.4 = (bf16[256,3072]{1,0:T(8,128)(2,1)S(1)}, bf16[256,3072]{1,0:T(8,128)(2,1)}, u32[]{:S(2)}) copy-start(bf16[256,3072]{1,0:T(8,128)(2,1)} %param.14) | copy-start | bytes 4718596
  7.2 230.2 %all-gather.4.cloned.1.call-start = ((), (), s32[]{:S(2)}) async-start(), calls=%async_computation.3 | async-start | bytes 2621440 | tf_op jit(solution)/shard_map/all_gather | solution.py:131
  7.9 240.1 %all-gather.6.cloned.1.call-start = ((), (), s32[]{:S(2)}) async-start(), calls=%async_computation.4 | async-start | bytes 7864320 | tf_op jit(solution)/shard_map/all_gather | solution.py:136
  8.7 86.9 %collective-permute-start = (bf16[256,3072]{1,0:T(8,128)(2,1)}, bf16[256,3072]{1,0:T(8,128)(2,1)S(1)}, u32[]{:S(2)}, u32[]{:S(2)}) collective-permute-start(bf16[256,3072]{1,0:T(8,128)(2,1)} %param.14), channel_id=1, source_target_pairs={{0,1},{1,2},{2,3},{3,0},{4,5},{5,6},{6,7},{7,4},{8,9},{9,10},{10,1... | collective-permute-start | bytes 4718600 | tf_op jit(solution)/shard_map/ppermute | solution.py:19
  10.3 114.6 %collective-permute-start.1 = (bf16[256,3072]{1,0:T(8,128)(2,1)}, bf16[256,3072]{1,0:T(8,128)(2,1)}, u32[]{:S(2)}, u32[]{:S(2)}) collective-permute-start(bf16[256,3072]{1,0:T(8,128)(2,1)} %param.14), channel_id=1, source_target_pairs={{0,3},{1,0},{2,1},{3,2},{4,7},{5,4},{6,5},{7,6},{8,11},{9,8},{10,9... | collective-permute-start | bytes 4718600 | tf_op jit(solution)/shard_map/ppermute | solution.py:22
  95.6 122.5 %collective-permute-start.2 = (bf16[256,3072]{1,0:T(8,128)(2,1)S(1)}, bf16[256,3072]{1,0:T(8,128)(2,1)S(1)}, u32[]{:S(2)}, u32[]{:S(2)}) collective-permute-start(bf16[256,3072]{1,0:T(8,128)(2,1)S(1)} %collective-permute-done), channel_id=1, source_target_pairs={{0,1},{1,2},{2,3},{3,0},{4,5},{5,6},{6,7},{7,4},{8,9},{9,10},{10,1... | collective-permute-start | bytes 4718600 | tf_op jit(solution)/shard_map/ppermute | solution.py:19
  221.2 5.8 %collective-permute-start.3 = (bf16[128,2048]{0,1:T(8,128)(2,1)}, bf16[128,2048]{0,1:T(8,128)(2,1)}, u32[]{:S(2)}, u32[]{:S(2)}) collective-permute-start(bf16[128,2048]{0,1:T(8,128)(2,1)} %bitcast.4), channel_id=1, source_target_pairs={{0,4},{4,8},{8,12},{1,5},{5,9},{9,13},{2,6},{6,10},{10,14},{3,7},{... | collective-permute-start | bytes 1572872 | tf_op jit(solution)/shard_map/ppermute | solution.py:32
  224.3 4.6 collective-permute-start.4
  235.0 2.4 copy-start
  239.9 13.9 %copy-start.2 = (bf16[256,1024]{1,0:T(8,128)(2,1)}, bf16[256,1024]{1,0:T(8,128)(2,1)S(1)}, u32[]{:S(2)}) copy-start(bf16[256,1024]{1,0:T(8,128)(2,1)S(1)} %get-tuple-element.97) | copy-start | bytes 1572868
  297.3 9.2 %all-to-all-start = ((bf16[4,8,128]{2,1,0:T(8,128)(2,1)}), bf16[4,8,128]{2,1,0:T(8,128)(2,1)S(1)}, u32[]{:S(2)}, u32[]{:S(2)}) async-start(bf16[4,8,128]{2,1,0:T(8,128)(2,1)} %broadcast_in_dim.90), calls=%async_computation | async-start | bytes 16384 | tf_op jit(solution)/shard_map/all_to_all | solution.py:149
  302.3 80.2 %all-gather.8.cloned.1.call-start = ((), (), s32[]{:S(2)}) async-start(), calls=%async_computation.5 | async-start | bytes 2621440 | tf_op jit(solution)/shard_map/all_gather | solution.py:156
  322.9 7.3 %copy-start.6 = (u32[32]{0:T(128)S(1)}, u32[32]{0:T(128)}, u32[]{:S(2)}) copy-start(u32[32]{0:T(128)} %constant.111) | copy-start | bytes 388
  323.0 8.6 %copy-start.5 = (s32[2,128]{1,0:T(2,128)S(1)}, s32[2,128]{1,0:T(2,128)}, u32[]{:S(2)}) copy-start(s32[2,128]{1,0:T(2,128)} %param.12) | copy-start | bytes 3076
  323.0 59.5 %copy-start.3 = (bf16[256,1024]{1,0:T(8,128)(2,1)S(1)}, bf16[256,1024]{1,0:T(8,128)(2,1)}, u32[]{:S(2)}) copy-start(bf16[256,1024]{1,0:T(8,128)(2,1)} %copy-done.2) | copy-start | bytes 1572868
  325.4 54.8 %all-to-all-start.2 = ((bf16[4,2,32768]{2,1,0:T(2,128)(2,1)}), bf16[4,2,32768]{2,1,0:T(2,128)(2,1)S(1)}, u32[]{:S(2)}, u32[]{:S(2)}) async-start(bf16[4,2,32768]{2,1,0:T(2,128)(2,1)} %reshape.161), calls=%async_computation.2 | async-start | bytes 1048576 | tf_op jit(solution)/shard_map/all_to_all | solution.py:152
  330.3 144.9 %all-reduce.4.cloned.1.call-start = ((), (), s32[]{:S(2)}) async-start(), calls=%async_computation.6 | async-start | bytes 262144
  384.8 91.8 %copy-start.1 = (bf16[256,1024]{1,0:T(8,128)(2,1)}, bf16[256,1024]{1,0:T(8,128)(2,1)S(1)}, u32[]{:S(2)}) copy-start(bf16[256,1024]{1,0:T(8,128)(2,1)S(1)} %fusion.19) | copy-start | bytes 1572868
Sparse Core Ops, SparseCore 0:
  9.6 87.1 all-gather.3
  98.3 149.5 all-gather.5
  304.7 54.9 all-gather.7
  385.8 89.3 all-reduce.3
